TPU v7x, 256 devices: a whole 4x4x8 slice. The times are simulated.
256 devices in a mesh: ctx: 8 (over x, y_lo), chan: 32 (over z, y_hi, core).
Axes of the slice: x: 4, y: 4 (y_hi: 2, y_lo: 2; y = y_hi * 2 + y_lo), z: 8, core: 2. Of those that a mesh axis runs over, the one named last changes fastest.
Arguments:
- gate_input: bfloat16 [1024, 8192], P('ctx', 'chan'), may hold values from -6 to 6
- key_input: bfloat16 [1024, 8192], P('ctx', 'chan'), may hold values from -6 to 6
- value_input: bfloat16 [1024, 8192], P('ctx', 'chan'), may hold values from -6 to 6
- short_filters: float32 [3, 7, 8192], P(None, None, 'chan'), may hold values from -2.5 to 2.5
- pole_time: float32 [8192, 16], P('chan'), may hold values from 30 to 2048
- residues: float32 [8192, 16], P('chan'), may hold values from -1.5 to 1.5
- out_weight: bfloat16 [8192, 8192], P('ctx', 'chan'), may hold values from -0.125 to 0.125
- out_cotangent: bfloat16 [1024, 8192], P('ctx', 'chan'), may hold values from -6 to 6
Outputs:
- block_output: bfloat16 [1024, 8192], P('ctx', 'chan')
- gate_grad: bfloat16 [1024, 8192], P('ctx', 'chan')
- key_grad: bfloat16 [1024, 8192], P('ctx', 'chan')
- value_grad: bfloat16 [1024, 8192], P('ctx', 'chan')
All inputs are finite; a program needn't handle non-finite values.
Results may differ from a plain program's by a relative error of at most 0.0049.
Values may be sent and summed in bfloat16 or wider, within the bound.
No kernel may reach another device: no remote copies, remote signals or barrier semaphores. Data moves between devices by JAX's collectives and lax.ppermute only.
A program may use at most 64 MiB of HBM per device.

v0:
```python
import math
import jax
import jax.numpy as jnp
from jax import lax
from jax.sharding import PartitionSpec as P

HIGHEST = lax.Precision.HIGHEST


def from_behind(block, axis, distance):
    devices = range(lax.axis_size(axis))
    route = [(i - distance, i) for i in devices if i - distance in devices]
    return lax.ppermute(block, axis, route)


def carried_in(x, axis, combine, identity, reverse):
    peers, position = (lax.axis_size(axis), lax.axis_index(axis))
    everything = jax.tree.map(lambda part: lax.all_gather(part, axis), x)
    start = jax.tree.map(
        lambda part, zero: jnp.broadcast_to(jnp.asarray(zero, part.dtype), part.shape), x, identity
    )

    def lap(k, before):
        at = peers - 1 - k if reverse else k
        reached = at > position if reverse else at < position
        new = combine(before, jax.tree.map(lambda part: part[at], everything))
        return jax.tree.map(lambda a, b: jnp.where(reached, a, b), new, before)

    return lax.fori_loop(0, peers, lap, start)


def causal_taps(extended, filter_taps, length):
    tap_count = filter_taps.shape[0]
    summed = jnp.zeros((length, extended.shape[1]), jnp.float32)
    for offset in range(tap_count):
        lead_row = tap_count - 1 - offset
        summed = summed + filter_taps[offset][None, :] * extended[lead_row : lead_row + length]
    return summed


def anti_taps(extended, filter_taps, length):
    tap_count = filter_taps.shape[0]
    summed = jnp.zeros((length, extended.shape[1]), jnp.float32)
    for offset in range(tap_count):
        summed = summed + filter_taps[offset][None, :] * extended[offset : offset + length]
    return summed


def spectral_tables(length):
    doubled = 2 * length
    freqs = lax.broadcasted_iota(jnp.int32, (doubled, length), 0)
    places = lax.broadcasted_iota(jnp.int32, (doubled, length), 1)
    angles = (freqs * places % doubled).astype(jnp.float32) * (2.0 * math.pi / doubled)
    forward = jnp.concatenate([jnp.cos(angles), -jnp.sin(angles)], axis=0)
    inverse = forward.T / doubled
    return (forward, inverse)


def apply_filter(spectrum, signal, forward, inverse):
    middle = forward.shape[0] // 2
    spectra = jnp.dot(forward, signal, precision=HIGHEST)
    real_sig = spectra[:middle]
    imag_sig = spectra[middle:]
    real_filt = spectrum[:middle]
    imag_filt = spectrum[middle:]
    product = jnp.concatenate(
        [real_sig * real_filt - imag_sig * imag_filt, real_sig * imag_filt + imag_sig * real_filt],
        axis=0,
    )
    return jnp.dot(inverse, product, precision=HIGHEST)


def mode_sums(inv_time, modal_weight, mixed, grad_long, length):
    offsets = lax.broadcasted_iota(jnp.float32, (length, 1), 0)

    def one_mode(carry, pieces):
        rate_row, weight_row = pieces
        decay = jnp.exp(-offsets * rate_row[None, :])
        forward_sum = jnp.sum(decay[::-1] * mixed, axis=0)
        backward_sum = jnp.sum(decay * grad_long, axis=0)
        return (carry + weight_row[None, :] * decay, (forward_sum, backward_sum))

    start_filter = jnp.zeros((length, mixed.shape[1]), jnp.float32)
    filt_table, sums_pair = lax.scan(one_mode, start_filter, (inv_time, modal_weight))
    return (filt_table, sums_pair[0], sums_pair[1])


def mode_terms(inv_time, modal_weight, state_in, state_back, length):
    offsets = lax.broadcasted_iota(jnp.float32, (length, 1), 0)

    def one_mode(carry, pieces):
        rate_row, weight_row, enter_row, back_row = pieces
        decay = jnp.exp(-offsets * rate_row[None, :])
        step_decay = (weight_row * jnp.exp(-rate_row))[None, :]
        ahead = step_decay * decay * enter_row[None, :]
        behind = step_decay * decay[::-1] * back_row[None, :]
        return ((carry[0] + ahead, carry[1] + behind), None)

    start_terms = jnp.zeros((length, inv_time.shape[1]), jnp.float32)
    result_pair, _ = lax.scan(
        one_mode, (start_terms, start_terms), (inv_time, modal_weight, state_in, state_back)
    )
    return (result_pair[0], result_pair[1])


def chain_combine(earlier, later):
    return (earlier[0] * later[0], later[0] * earlier[1] + later[1])


def body(
    gate_input,
    key_input,
    value_input,
    short_filters,
    pole_time,
    residues,
    out_weight,
    out_cotangent,
):
    length = gate_input.shape[0]
    tap_count = short_filters.shape[1]
    stacked = jnp.stack([gate_input, key_input, value_input])
    tails = from_behind(stacked[:, length - (tap_count - 1) :, :], "ctx", 1)
    extended = jnp.concatenate([tails, stacked], axis=1).astype(jnp.float32)
    gate_short = causal_taps(extended[0], short_filters[0], length)
    key_short = causal_taps(extended[1], short_filters[1], length)
    value_short = causal_taps(extended[2], short_filters[2], length)
    mixed = key_short * value_short
    weight_full = lax.all_gather(out_weight, "ctx", axis=0, tiled=True)
    row_block = weight_full
    grad_gated = lax.psum_scatter(
        lax.dot_general(
            row_block, out_cotangent, (((1,), (1,)), ((), ())), preferred_element_type=jnp.float32
        ),
        "chan",
        scatter_dimension=0,
        tiled=True,
    ).T
    grad_long = grad_gated * gate_short
    inv_time = 1.0 / pole_time.T
    modal_weight = residues.T * jnp.sqrt(-jnp.expm1(-2.0 * inv_time))
    filt_table, forward_sums, backward_sums = mode_sums(
        inv_time, modal_weight, mixed, grad_long, length
    )
    block_decay = jnp.exp(-float(length) * inv_time)
    identity = (jnp.ones_like(block_decay), jnp.zeros_like(block_decay))
    state_in = carried_in((block_decay, forward_sums), "ctx", chain_combine, identity, False)[1]
    state_back = carried_in((block_decay, backward_sums), "ctx", chain_combine, identity, True)[1]
    forward, inverse = spectral_tables(length)
    spectrum = jnp.dot(forward, filt_table, precision=HIGHEST)
    long_local = apply_filter(spectrum, mixed, forward, inverse)
    back_local = apply_filter(spectrum, grad_long[::-1], forward, inverse)[::-1]
    ahead_terms, behind_terms = mode_terms(inv_time, modal_weight, state_in, state_back, length)
    long_out = long_local + ahead_terms
    grad_mixed = back_local + behind_terms
    gated = (gate_short * long_out).astype(jnp.bfloat16)
    row_block = weight_full
    block_output = jnp.dot(
        lax.all_gather(gated, "chan", axis=1, tiled=True),
        row_block,
        preferred_element_type=jnp.float32,
    ).astype(jnp.bfloat16)
    grad_gate_short = grad_gated * long_out
    grad_key_short = grad_mixed * value_short
    grad_value_short = grad_mixed * key_short
    grads = jnp.stack([grad_gate_short, grad_key_short, grad_value_short])
    heads = from_behind(grads[:, : tap_count - 1, :], "ctx", -1)
    ext_grads = jnp.concatenate([grads, heads], axis=1)
    gate_grad = anti_taps(ext_grads[0], short_filters[0], length).astype(jnp.bfloat16)
    key_grad = anti_taps(ext_grads[1], short_filters[1], length).astype(jnp.bfloat16)
    value_grad = anti_taps(ext_grads[2], short_filters[2], length).astype(jnp.bfloat16)
    return (block_output, gate_grad, key_grad, value_grad)


def solution(mesh):
    in_specs = (
        P("ctx", "chan"),
        P("ctx", "chan"),
        P("ctx", "chan"),
        P(None, None, "chan"),
        P("chan", None),
        P("chan", None),
        P("ctx", "chan"),
        P("ctx", "chan"),
    )
    out_specs = (P("ctx", "chan"), P("ctx", "chan"), P("ctx", "chan"), P("ctx", "chan"))
    return jax.shard_map(body, mesh=mesh, in_specs=in_specs, out_specs=out_specs, check_vma=False)
```

profile of v0, /device:TPU:1, one launch (start us, length us, event | category | flops | bytes accessed | tf_op | source)
XLA Modules:
  0.0 426.2 jit_solution(3915547119389081948)
XLA Ops:
  7.2 0.7 all-gather.6.cloned.1.call-update
  8.0 97.7 %all-gather.6.cloned.1.call-done = bf16[8192,256]{1,0:T(8,128)(2,1)} async-done(((bf16[1024,256]{1,0:T(8,128)(2,1)}), bf16[8192,256]{1,0:T(8,128)(2,1)}) %all-gather.6.cloned.1.call-update) | async-done | bytes 4194320 | tf_op jit(solution)/shard_map/all_gather | solution.py:129
  105.7 5.5 %fusion.119 = f32[8192,128]{1,0:T(8,128)} fusion(bf16[8192,256]{1,0:T(8,128)(2,1)} %all-gather.6.cloned.1.call-done, bf16[128,256]{1,0:T(8,128)(2,1)S(1)} %copy-done), kind=kOutput, calls=%fused_computation.197 | convolution fusion | flops 536870912 | bytes 8454144 | tf_op jit(solution)/shard_map/dot_general | solution.py:132
  111.2 0.7 copy-done.3
  112.3 0.1 pad_maximum_fusion.4
  112.5 1.5 collective-permute-start
  114.0 0.5 sine_negate_fusion
  114.6 25.4 %all-gather = f32[128,256]{1,0:T(8,128)} all-gather(f32[16,256]{1,0:T(8,128)S(1)} %get-tuple-element.639), channel_id=2, replica_groups=mesh['ctx'=8,'chan'=32] {'ctx'}, dimensions={0}, use_global_device_ids=true | all-gather | bytes 147456 | tf_op jit(solution)/shard_map/all_gather | solution.py:18
  140.1 0.2 maximum_convert_fusion
  140.3 0.9 fusion.114
  141.3 0.6 fusion.103
  141.9 93.7 %reduce-scatter.2.cloned.1.call-done = f32[256,128]{1,0:T(8,128)} async-done(((f32[8192,128]{1,0:T(8,128)}), f32[256,128]{1,0:T(8,128)}) %reduce-scatter.2.cloned.1.call-update) | async-done | bytes 131088 | tf_op jit(solution)/shard_map/reduce_scatter | solution.py:131
  235.6 2.1 bitcast_multiply_fusion.3
  237.6 0.2 rev.16
  237.9 0.6 fusion.101
  238.5 6.3 %while.62 = (s32[]{:T(128)}, f32[128,256]{1,0:T(8,128)S(1)}, f32[16,256]{1,0:T(8,128)S(1)}, f32[16,256]{1,0:T(8,128)S(1)}, f32[16,256]{1,0:T(8,128)S(1)}, /*inde...) while((s32[]{:T(128)}, f32[128,256]{1,0:T(8,128)S(1)}, ...), condition=%wide.region_4.5_spmd.clone, body=%wide.region_1.4_spmd.clone.sunk | while | flops 261763 | bytes 1062019 | solution.py:84
  238.6 0.1 multiply_reduce_fusion.4
  239.0 0.1 multiply_reduce_fusion.4
  239.4 0.1 multiply_reduce_fusion.4
  239.7 0.1 multiply_reduce_fusion.4
  240.1 0.1 multiply_reduce_fusion.4
  240.5 0.1 multiply_reduce_fusion.4
  241.3 0.1 multiply_reduce_fusion.4
  241.7 0.1 multiply_reduce_fusion.4
  242.1 0.1 multiply_reduce_fusion.4
  242.5 0.1 multiply_reduce_fusion.4
  242.9 0.1 multiply_reduce_fusion.4
  244.1 0.1 multiply_reduce_fusion.4
  244.5 0.1 multiply_reduce_fusion.4
  244.8 0.6 fusion.102
  245.5 1.0 fusion.9
  246.5 0.2 rev.17
  246.7 21.8 %all-gather.1 = f32[128,256]{1,0:T(8,128)S(1)} all-gather(f32[16,256]{1,0:T(8,128)S(1)} %get-tuple-element.433), channel_id=3, replica_groups=mesh['ctx'=8,'chan'=32] {'ctx'}, dimensions={0}, use_global_device_ids=true | all-gather | bytes 147456 | tf_op jit(solution)/shard_map/all_gather | solution.py:18
  268.6 5.8 %while.63 = (s32[]{:T(128)}, f32[16,256]{1,0:T(8,128)S(1)}, s32[]{:T(128)}, f32[8,16,256]{2,1,0:T(8,128)}, f32[8,16,256]{2,1,0:T(8,128)S(1)}, /*index=5*/s32[]{:T(128)}, s32[]{:T(128)}) while((s32[]{:T(128)}, f32[16,256]{1,0:T(8,128)S(1)}, s32[]{:T(128)}, f32[8,16,256]{2,1,0:T(8,128)}, f32[8,16,256]{2,1,0:T(8,128)S(1)}, ...), condition=%wide.region_6.7_spmd.clone, body=%wide.region_5.6_spmd.clone.sunk | while | flops 16388 | bytes 65645 | solution.py:29
  268.6 0.7 fusion.129
  269.3 0.7 fusion.129
  270.0 0.7 fusion.129
  270.7 0.7 fusion.129
  271.5 0.7 fusion.129
  272.2 0.7 fusion.129
  272.9 0.7 fusion.129
  273.6 0.7 fusion.129
  274.4 21.8 %all-gather.2 = f32[128,256]{1,0:T(8,128)S(1)} all-gather(f32[16,256]{1,0:T(8,128)S(1)} %get-tuple-element.435), channel_id=4, replica_groups=mesh['ctx'=8,'chan'=32] {'ctx'}, dimensions={0}, use_global_device_ids=true | all-gather | bytes 147456 | tf_op jit(solution)/shard_map/all_gather | solution.py:18
  296.2 5.8 %while.64 = (s32[]{:T(128)}, f32[16,256]{1,0:T(8,128)S(1)}, s32[]{:T(128)}, f32[8,16,256]{2,1,0:T(8,128)}, f32[8,16,256]{2,1,0:T(8,128)S(1)}, /*index=5*/s32[]{:T(128)}, s32[]{:T(128)}, s32[]{:T(128)}, s32[]{:T(128)}) while((s32[]{:T(128)}, f32[16,256]{1,0:T(8,128)S(1)}, s32[]{:T(128)}, f32[8,16,256]{2,1,0:T(8,128)}, ...), condition=%wide.region_8.9_spmd.clone, body=%wide.region_7.8_spmd.clone.sunk | while | flops 16392 | bytes 65707 | solution.py:29
  296.2 0.7 fusion.130
  296.9 0.7 fusion.130
  297.6 0.7 fusion.130
  298.3 0.7 fusion.130
  299.1 0.7 fusion.130
  299.8 0.7 fusion.130
  300.5 0.7 fusion.130
  301.2 0.7 fusion.130
  302.0 5.4 %while.65 = (s32[]{:T(128)}, f32[128,256]{1,0:T(8,128)S(1)}, f32[128,256]{1,0:T(8,128)S(1)}, f32[16,256]{1,0:T(8,128)S(1)}, f32[16,256]{1,0:T(8,128)S(1)}, /*ind...) while((s32[]{:T(128)}, f32[128,256]{1,0:T(8,128)S(1)}, ...), condition=%wide.region_10.11_spmd.clone, body=%wide.region_9.10_spmd.clone.sunk | while | flops 295555 | bytes 1063032 | solution.py:100
  307.6 1.0 convolution_add_fusion
  308.7 1.3 collective-permute-start.1
  310.0 7.3 %collective-permute-done.1 = f32[3,6,256]{1,2,0:T(8,128)S(1)} collective-permute-done((f32[3,6,256]{1,2,0:T(8,128)S(1)}, f32[3,6,256]{1,2,0:T(8,128)S(1)}, u32[]{:S(2)}, u32[]{:S(2)}) %collective-permute-start.1) | collective-permute-done | bytes 18464 | tf_op jit(solution)/shard_map/ppermute | solution.py:13
  317.4 1.1 fusion.46
  318.5 0.7 copy.21
  319.2 0.5 fusion.33
  319.7 0.7 copy.22
  320.5 0.5 fusion.20
  321.0 0.7 copy.23
  321.7 93.5 %all-gather.8.cloned.1.call-done = bf16[128,8192]{0,1:T(8,128)(2,1)} async-done(((bf16[128,256]{0,1:T(8,128)(2,1)}), bf16[128,8192]{0,1:T(8,128)(2,1)}) %all-gather.8.cloned.1.call-update) | async-done | bytes 2097168 | tf_op jit(solution)/shard_map/all_gather | solution.py:159
  415.2 4.4 %convolution_convert_fusion = bf16[128,256]{1,0:T(8,128)(2,1)} fusion(bf16[128,8192]{0,1:T(8,128)(2,1)} %all-gather.8.cloned.1.call-done, bf16[8192,256]{1,0:T(8,128)(2,1)} %all-gather.6.cloned.1.call-done), kind=kOutput, calls=%fused_computation.24 | convolution fusion | flops 536903680 | bytes 6356992 | tf_op jit(solution)/shard_map/dot_general | solution.py:158
  (242 shorter events, 9.5 us)
Async XLA Ops:
  7.2 98.5 %copy-start = (bf16[128,256]{1,0:T(8,128)(2,1)S(1)}, bf16[128,256]{1,0:T(8,128)(2,1)}, u32[]{:S(2)}) copy-start(bf16[128,256]{1,0:T(8,128)(2,1)} %param.23) | copy-start | bytes 196612
  7.2 98.5 %all-gather.6.cloned.1.call-start = ((), (), s32[]{:S(2)}) async-start(), calls=%async_computation.1 | async-start | bytes 4718592 | tf_op jit(solution)/shard_map/all_gather | solution.py:129
  7.9 227.7 %reduce-scatter.2.cloned.1.call-start = ((), (), s32[]{:S(2)}) async-start(), calls=%async_computation.2 | async-start | bytes 4325376 | tf_op jit(solution)/shard_map/reduce_scatter | solution.py:131
  111.1 0.8 copy-start.3
  111.1 1.0 copy-start.4
  111.1 1.1 copy-start.5
  111.1 3.4 copy-start.7
  111.1 3.4 copy-start.6
  111.1 3.4 copy-start.8
  111.2 304.0 %all-gather.8.cloned.1.call-start = ((), (), s32[]{:S(2)}) async-start(), calls=%async_computation.3 | async-start | bytes 2162688 | tf_op jit(solution)/shard_map/all_gather | solution.py:159
  112.5 27.6 %collective-permute-start = (bf16[3,6,256]{1,2,0:T(8,128)(2,1)S(1)}, bf16[3,6,256]{1,2,0:T(8,128)(2,1)S(1)}, u32[]{:S(2)}, u32[]{:S(2)}) collective-permute-start(bf16[3,6,256]{1,2,0:T(8,128)(2,1)S(1)} %pad_maximum_fusion.4), channel_id=1, source_target_pairs={{0,32},{32,64},{64,96},{96,128},{128,160},{160,192},{192,224},{1,3... | collective-permute-start | bytes 27656 | tf_op jit(solution)/shard_map/ppermute | solution.py:13
  301.9 6.6 %copy-start.1 = (f32[256,128]{1,0:T(8,128)S(1)}, f32[256,128]{1,0:T(8,128)}, u32[]{:S(2)}) copy-start(f32[256,128]{1,0:T(8,128)} %reduce-scatter.2.cloned.1.call-done) | copy-start | bytes 393220
  302.0 15.4 %copy-start.2 = (f32[128,256]{0,1:T(8,128)S(1)}, f32[128,256]{0,1:T(8,128)}, u32[]{:S(2)}) copy-start(f32[128,256]{0,1:T(8,128)} %get-tuple-element.595) | copy-start | bytes 393220
  308.7 8.6 %collective-permute-start.1 = (f32[3,6,256]{1,2,0:T(8,128)S(1)}, f32[3,6,256]{1,2,0:T(8,128)S(1)}, u32[]{:S(2)}, u32[]{:S(2)}) collective-permute-start(f32[3,6,256]{1,2,0:T(8,128)S(1)} %pad_maximum_fusion.1), channel_id=1, source_target_pairs={{32,0},{64,32},{96,64},{128,96},{160,128},{192,160},{224,192},{33,... | collective-permute-start | bytes 55304 | tf_op jit(solution)/shard_map/ppermute | solution.py:13
Sparse Core Ops, SparseCore 0:
  9.8 95.8 all-gather.5
  111.3 124.2 reduce-scatter.1
  318.6 96.5 all-gather.7
where the time goes:
time: 428 us; the launch traced here: 426 us
  waiting for transfers between devices  293 us (68%)
  blocking collectives  69 us (16%)
  other arithmetic  23.4 us (5%)
  between operations  14.1 us (3%)
  matrix products  13.6 us (3%)
  local copies, waits for them, and re-layouts  8.38 us (2%)
    all_gather x1, waiting for transfers between devices, body(): weight_full = lax.all_gather(out_weight, 'ctx', axis=0, tiled=True)  97.7 us
    reduce_scatter x1, waiting for transfers between devices, body(): lax.psum_scatter(lax.dot_general(row_block, out_cotangent, (((1,), (1,)),...  93.7 us
    all_gather x1, waiting for transfers between devices, body(): lax.all_gather(gated, 'chan', axis=1, tiled=True)  93.5 us
    all_gather x3, blocking collectives, carried_in(): everything = jax.tree.map(lambda part: lax.all_gather(part, axis), x)  69 us
    select_n x16, other arithmetic, lap(): return jax.tree.map(lambda a, b: jnp.where(reached, a, b), new, before)  11.6 us
  transfers between devices with their start and end apart: 5, of which 4 were waited for; matrix products, arithmetic and copies ran while one was open for 1% of the time, Pallas kernels for 0%

commit v1 on v0

--- a/solution.py
+++ b/solution.py
@@ -156,7 +156,9 @@
     gated = (gate_short * long_out).astype(jnp.bfloat16)
     row_block = weight_full
     block_output = jnp.dot(
-        lax.all_gather(gated, "chan", axis=1, tiled=True),
+        jnp.concatenate(
+            lax.all_to_all(jnp.stack([gated] * lax.axis_size("chan")), "chan", 0, 0), axis=1
+        ),
         row_block,
         preferred_element_type=jnp.float32,
     ).astype(jnp.bfloat16)

time: 428 us -> 416 us (0.972)
  waiting for transfers between devices: 293 us -> 247 us
  starting transfers between devices: 2.91 us -> 28.3 us
  local copies, waits for them, and re-layouts: 8.38 us -> 30.8 us
  other arithmetic: 23.4 us -> 11.3 us
    all_gather x1 -> x0, waiting for transfers between devices: 93.5 us -> none  [body(): lax.all_gather(gated, 'chan', axis=1, tiled=True)]
    all_to_all x0 -> x1, waiting for transfers between devices: none -> 46.1 us  [body(): lax.all_to_all(jnp.stack([gated] * lax.axis_size('chan')), 'chan', 0, 0)]
    all_to_all x0 -> x1, starting transfers between devices: none -> 25.4 us  [body(): lax.all_to_all(jnp.stack([gated] * lax.axis_size('chan')), 'chan', 0, 0)]
    dynamic_update_slice x32, local copies, waits for them, and re-layouts: 1.36 us -> 21.7 us  [mode_sums(): lax.scan(one_mode, start_filter, (inv_time, modal_weight))]
    select_n x16, other arithmetic: 11.6 us -> 0.18 us  [lap(): return jax.tree.map(lambda a, b: jnp.where(reached, a, b), new, before)]
  transfers between devices with their start and end apart: 5 -> 5, of which waited for: 4 -> 4; matrix products, arithmetic and copies ran while one was open for 1% -> 2% of each run, Pallas kernels for 0% -> 0%
where the time goes in v1:
time: 416 us; the launch traced here: 414 us
  waiting for transfers between devices  247 us (59%)
  blocking collectives  66.8 us (16%)
  local copies, waits for them, and re-layouts  30.8 us (7%)
  starting transfers between devices  28.3 us (7%)
  between operations  15 us (4%)
  matrix products  13 us (3%)
  other arithmetic  11.3 us (3%)
    all_gather x1, waiting for transfers between devices, body(): weight_full = lax.all_gather(out_weight, 'ctx', axis=0, tiled=True)  97.7 us
    reduce_scatter x1, waiting for transfers between devices, body(): lax.psum_scatter(lax.dot_general(row_block, out_cotangent, (((1,), (1,)),...  95.6 us
    all_gather x3, blocking collectives, carried_in(): everything = jax.tree.map(lambda part: lax.all_gather(part, axis), x)  66.8 us
    all_to_all x1, waiting for transfers between devices, body(): lax.all_to_all(jnp.stack([gated] * lax.axis_size('chan')), 'chan', 0, 0)  46.1 us
    all_to_all x1, starting transfers between devices, body(): lax.all_to_all(jnp.stack([gated] * lax.axis_size('chan')), 'chan', 0, 0)  25.4 us
    dynamic_update_slice x32, local copies, waits for them, and re-layouts, mode_sums(): lax.scan(one_mode, start_filter, (inv_time, modal_weight))  21.7 us
  transfers between devices with their start and end apart: 5, of which 4 were waited for; matrix products, arithmetic and copies ran while one was open for 2% of the time, Pallas kernels for 0%

profile of v1, /device:TPU:1, one launch (start us, length us, event | category | flops | bytes accessed | tf_op | source)
XLA Modules:
  0.0 414.4 jit_solution(10993899141801166496)
XLA Ops:
  7.2 0.7 all-gather.5.cloned.1.call-update
  8.0 97.7 %all-gather.5.cloned.1.call-done = bf16[8192,256]{1,0:T(8,128)(2,1)} async-done(((bf16[1024,256]{1,0:T(8,128)(2,1)}), bf16[8192,256]{1,0:T(8,128)(2,1)}) %all-gather.5.cloned.1.call-update) | async-done | bytes 4194320 | tf_op jit(solution)/shard_map/all_gather | solution.py:129
  105.7 5.5 %fusion.119 = f32[8192,128]{1,0:T(8,128)} fusion(bf16[8192,256]{1,0:T(8,128)(2,1)} %all-gather.5.cloned.1.call-done, bf16[128,256]{1,0:T(8,128)(2,1)S(1)} %copy-done), kind=kOutput, calls=%fused_computation.197 | convolution fusion | flops 536870912 | bytes 8454144 | tf_op jit(solution)/shard_map/dot_general | solution.py:132
  111.2 0.8 copy-done.2
  112.3 0.1 pad_maximum_fusion.4
  112.4 1.5 collective-permute-start
  114.0 0.5 sine_negate_fusion
  114.8 23.1 %all-gather = f32[128,256]{1,0:T(8,128)S(1)} all-gather(f32[16,256]{1,0:T(8,128)S(1)} %get-tuple-element.651), channel_id=2, replica_groups=mesh['ctx'=8,'chan'=32] {'ctx'}, dimensions={0}, use_global_device_ids=true | all-gather | bytes 147456 | tf_op jit(solution)/shard_map/all_gather | solution.py:18
  138.0 0.2 maximum_convert_fusion
  138.2 0.9 fusion.114
  139.4 0.6 fusion.103
  139.9 95.6 %reduce-scatter.2.cloned.1.call-done = f32[256,128]{1,0:T(8,128)} async-done(((f32[8192,128]{1,0:T(8,128)}), f32[256,128]{1,0:T(8,128)}) %reduce-scatter.2.cloned.1.call-update) | async-done | bytes 131088 | tf_op jit(solution)/shard_map/reduce_scatter | solution.py:131
  235.6 1.4 bitcast_multiply_fusion.3
  237.0 0.2 rev.16
  237.3 0.6 fusion.101
  237.9 26.1 %while.62 = (s32[]{:T(128)}, f32[128,256]{1,0:T(8,128)S(1)}, f32[16,256]{1,0:T(8,128)S(1)}, f32[16,256]{1,0:T(8,128)}, f32[16,256]{1,0:T(8,128)S(1)}, /*index=5*...) while((s32[]{:T(128)}, f32[128,256]{1,0:T(8,128)S(1)}, ...), condition=%wide.region_4.5_spmd.clone, body=%wide.region_1.4_spmd.clone.sunk | while | flops 261763 | bytes 1062019 | solution.py:84
  238.0 0.1 multiply_reduce_fusion.4
  238.3 1.3 dynamic_update_slice.16
  239.6 0.1 multiply_reduce_fusion.4
  239.9 1.3 dynamic_update_slice.16
  241.2 0.1 multiply_reduce_fusion.4
  241.5 1.3 dynamic_update_slice.16
  242.9 0.1 multiply_reduce_fusion.4
  243.2 1.3 dynamic_update_slice.16
  244.5 0.1 multiply_reduce_fusion.4
  244.8 1.3 dynamic_update_slice.16
  246.1 0.1 multiply_reduce_fusion.4
  246.4 1.3 dynamic_update_slice.16
  247.8 0.1 multiply_reduce_fusion.4
  248.1 1.3 dynamic_update_slice.16
  249.7 1.3 dynamic_update_slice.16
  251.3 1.3 dynamic_update_slice.16
  252.7 0.1 multiply_reduce_fusion.4
  253.0 1.3 dynamic_update_slice.16
  254.6 1.3 dynamic_update_slice.16
  255.9 0.1 multiply_reduce_fusion.4
  256.2 1.3 dynamic_update_slice.16
  257.8 1.3 dynamic_update_slice.16
  259.5 1.3 dynamic_update_slice.16
  260.8 0.1 multiply_reduce_fusion.4
  261.1 1.3 dynamic_update_slice.16
  262.7 1.3 dynamic_update_slice.16
  264.1 0.6 fusion.102
  264.6 0.1 multiply_subtract_fusion
  264.8 1.0 fusion.9
  265.8 0.2 rev.17
  265.9 21.8 %all-gather.1 = f32[128,256]{1,0:T(8,128)S(1)} all-gather(f32[16,256]{1,0:T(8,128)S(1)} %get-tuple-element.433), channel_id=3, replica_groups=mesh['ctx'=8,'chan'=32] {'ctx'}, dimensions={0}, use_global_device_ids=true | all-gather | bytes 147456 | tf_op jit(solution)/shard_map/all_gather | solution.py:18
  287.8 0.3 while.63
  288.1 21.9 %all-gather.2 = f32[128,256]{1,0:T(8,128)S(1)} all-gather(f32[16,256]{1,0:T(8,128)S(1)} %copy-done.7), channel_id=4, replica_groups=mesh['ctx'=8,'chan'=32] {'ctx'}, dimensions={0}, use_global_device_ids=true | all-gather | bytes 147456 | tf_op jit(solution)/shard_map/all_gather | solution.py:18
  309.9 0.3 while.64
  310.4 5.4 %while.65 = (s32[]{:T(128)}, f32[128,256]{1,0:T(8,128)S(1)}, f32[128,256]{1,0:T(8,128)S(1)}, f32[16,256]{1,0:T(8,128)S(1)}, f32[16,256]{1,0:T(8,128)S(1)}, /*ind...) while((s32[]{:T(128)}, f32[128,256]{1,0:T(8,128)S(1)}, ...), condition=%wide.region_10.11_spmd.clone, body=%wide.region_9.10_spmd.clone.sunk | while | flops 295555 | bytes 1063032 | solution.py:100
  316.0 1.0 convolution_add_fusion
  317.1 1.3 collective-permute-start.1
  318.4 7.4 %collective-permute-done.1 = f32[3,6,256]{1,2,0:T(8,128)S(1)} collective-permute-done((f32[3,6,256]{1,2,0:T(8,128)S(1)}, f32[3,6,256]{1,2,0:T(8,128)S(1)}, u32[]{:S(2)}, u32[]{:S(2)}) %collective-permute-start.1) | collective-permute-done | bytes 18464 | tf_op jit(solution)/shard_map/ppermute | solution.py:13
  325.9 0.5 fusion.46
  326.5 1.8 stack.22
  328.3 25.4 %all-to-all-start = ((bf16[32,128,256]{1,2,0:T(8,128)(2,1)}), bf16[32,128,256]{1,2,0:T(8,128)(2,1)S(1)}, u32[]{:S(2)}, u32[]{:S(2)}) async-start(bf16[32,128,256]{1,2,0:T(8,128)(2,1)} %stack.22), calls=%async_computation.1 | async-start | bytes 4194304 | tf_op jit(solution)/shard_map/all_to_all | solution.py:160
  353.7 0.7 copy.34
  354.5 1.2 fusion.33
  355.7 0.7 copy.35
  356.4 0.5 fusion.20
  357.0 0.7 copy.36
  357.7 46.1 %all-to-all-done = bf16[32,128,256]{1,2,0:T(8,128)(2,1)S(1)} async-done(((bf16[32,128,256]{1,2,0:T(8,128)(2,1)}), bf16[32,128,256]{1,2,0:T(8,128)(2,1)S(1)}, u32[]{:S(2)}, u32[]{:S(2)}) %all-to-all-start) | async-done | bytes 2097184 | tf_op jit(solution)/shard_map/all_to_all | solution.py:160
  403.8 3.8 convolution_convert_fusion
  (320 shorter events, 9.3 us)
Async XLA Ops:
  7.2 98.5 %copy-start = (bf16[128,256]{1,0:T(8,128)(2,1)S(1)}, bf16[128,256]{1,0:T(8,128)(2,1)}, u32[]{:S(2)}) copy-start(bf16[128,256]{1,0:T(8,128)(2,1)} %param.23) | copy-start | bytes 196612
  7.2 98.5 %all-gather.5.cloned.1.call-start = ((), (), s32[]{:S(2)}) async-start(), calls=%async_computation.2 | async-start | bytes 4718592 | tf_op jit(solution)/shard_map/all_gather | solution.py:129
  7.9 227.7 %reduce-scatter.2.cloned.1.call-start = ((), (), s32[]{:S(2)}) async-start(), calls=%async_computation.3 | async-start | bytes 4325376 | tf_op jit(solution)/shard_map/reduce_scatter | solution.py:131
  111.1 0.8 copy-start.2
  111.1 1.0 copy-start.3
  111.1 1.1 copy-start.4
  111.1 3.4 copy-start.6
  111.1 3.5 copy-start.5
  111.1 3.7 copy-start.8
  112.4 25.5 %collective-permute-start = (bf16[3,6,256]{1,2,0:T(8,128)(2,1)S(1)}, bf16[3,6,256]{1,2,0:T(8,128)(2,1)S(1)}, u32[]{:S(2)}, u32[]{:S(2)}) collective-permute-start(bf16[3,6,256]{1,2,0:T(8,128)(2,1)S(1)} %pad_maximum_fusion.4), channel_id=1, source_target_pairs={{0,32},{32,64},{64,96},{96,128},{128,160},{160,192},{192,224},{1,3... | collective-permute-start | bytes 27656 | tf_op jit(solution)/shard_map/ppermute | solution.py:13
  114.5 24.7 %copy-start.30 = (f32[1,1,256]{2,1,0:T(1,128)}, f32[1,1,256]{2,1,0:T(1,128)S(1)}, u32[]{:S(2)}) copy-start(f32[1,1,256]{2,1,0:T(1,128)S(1)} %get-tuple-element.649) | copy-start | bytes 3076
  114.5 24.7 %copy-start.32 = (f32[1,1,256]{2,1,0:T(1,128)}, f32[1,1,256]{2,1,0:T(1,128)S(1)}, u32[]{:S(2)}) copy-start(f32[1,1,256]{2,1,0:T(1,128)S(1)} %get-tuple-element.650) | copy-start | bytes 3076
  114.6 24.7 %copy-start.9 = (f32[1,1,256]{2,1,0:T(1,128)}, f32[1,1,256]{2,1,0:T(1,128)S(1)}, u32[]{:S(2)}) copy-start(f32[1,1,256]{2,1,0:T(1,128)S(1)} %get-tuple-element.631) | copy-start | bytes 3076
  114.6 24.7 %copy-start.11 = (f32[1,1,256]{2,1,0:T(1,128)}, f32[1,1,256]{2,1,0:T(1,128)S(1)}, u32[]{:S(2)}) copy-start(f32[1,1,256]{2,1,0:T(1,128)S(1)} %get-tuple-element.632) | copy-start | bytes 3076
  114.6 24.7 %copy-start.13 = (f32[1,1,256]{2,1,0:T(1,128)}, f32[1,1,256]{2,1,0:T(1,128)S(1)}, u32[]{:S(2)}) copy-start(f32[1,1,256]{2,1,0:T(1,128)S(1)} %get-tuple-element.633) | copy-start | bytes 3076
  114.6 24.7 %copy-start.15 = (f32[1,1,256]{2,1,0:T(1,128)}, f32[1,1,256]{2,1,0:T(1,128)S(1)}, u32[]{:S(2)}) copy-start(f32[1,1,256]{2,1,0:T(1,128)S(1)} %get-tuple-element.634) | copy-start | bytes 3076
  114.6 24.7 %copy-start.17 = (f32[1,1,256]{2,1,0:T(1,128)}, f32[1,1,256]{2,1,0:T(1,128)S(1)}, u32[]{:S(2)}) copy-start(f32[1,1,256]{2,1,0:T(1,128)S(1)} %get-tuple-element.635) | copy-start | bytes 3076
  114.6 24.7 %copy-start.19 = (f32[1,1,256]{2,1,0:T(1,128)}, f32[1,1,256]{2,1,0:T(1,128)S(1)}, u32[]{:S(2)}) copy-start(f32[1,1,256]{2,1,0:T(1,128)S(1)} %get-tuple-element.630) | copy-start | bytes 3076
  114.6 24.7 %copy-start.21 = (f32[1,1,256]{2,1,0:T(1,128)}, f32[1,1,256]{2,1,0:T(1,128)S(1)}, u32[]{:S(2)}) copy-start(f32[1,1,256]{2,1,0:T(1,128)S(1)} %get-tuple-element.636) | copy-start | bytes 3076
  114.6 24.7 %copy-start.23 = (f32[1,1,256]{2,1,0:T(1,128)}, f32[1,1,256]{2,1,0:T(1,128)S(1)}, u32[]{:S(2)}) copy-start(f32[1,1,256]{2,1,0:T(1,128)S(1)} %get-tuple-element.637) | copy-start | bytes 3076
  114.7 24.7 %copy-start.25 = (f32[1,1,256]{2,1,0:T(1,128)}, f32[1,1,256]{2,1,0:T(1,128)S(1)}, u32[]{:S(2)}) copy-start(f32[1,1,256]{2,1,0:T(1,128)S(1)} %get-tuple-element.638) | copy-start | bytes 3076
  114.7 24.7 %copy-start.27 = (f32[1,1,256]{2,1,0:T(1,128)}, f32[1,1,256]{2,1,0:T(1,128)S(1)}, u32[]{:S(2)}) copy-start(f32[1,1,256]{2,1,0:T(1,128)S(1)} %get-tuple-element.639) | copy-start | bytes 3076
  114.7 24.7 %copy-start.28 = (f32[1,1,256]{2,1,0:T(1,128)}, f32[1,1,256]{2,1,0:T(1,128)S(1)}, u32[]{:S(2)}) copy-start(f32[1,1,256]{2,1,0:T(1,128)S(1)} %get-tuple-element.640) | copy-start | bytes 3076
  114.7 24.7 %copy-start.29 = (f32[1,1,256]{2,1,0:T(1,128)}, f32[1,1,256]{2,1,0:T(1,128)S(1)}, u32[]{:S(2)}) copy-start(f32[1,1,256]{2,1,0:T(1,128)S(1)} %get-tuple-element.641) | copy-start | bytes 3076
  114.7 122.5 %copy-start.34 = (f32[1,1,256]{2,1,0:T(1,128)}, f32[1,1,256]{2,1,0:T(1,128)S(1)}, u32[]{:S(2)}) copy-start(f32[1,1,256]{2,1,0:T(1,128)S(1)} %get-tuple-element.642) | copy-start | bytes 3076
  114.7 122.5 %copy-start.36 = (f32[1,1,256]{2,1,0:T(1,128)}, f32[1,1,256]{2,1,0:T(1,128)S(1)}, u32[]{:S(2)}) copy-start(f32[1,1,256]{2,1,0:T(1,128)S(1)} %get-tuple-element.643) | copy-start | bytes 3076
  114.7 122.5 %copy-start.38 = (f32[1,1,256]{2,1,0:T(1,128)}, f32[1,1,256]{2,1,0:T(1,128)S(1)}, u32[]{:S(2)}) copy-start(f32[1,1,256]{2,1,0:T(1,128)S(1)} %get-tuple-element.644) | copy-start | bytes 3076
  114.7 122.5 %copy-start.40 = (f32[1,1,256]{2,1,0:T(1,128)}, f32[1,1,256]{2,1,0:T(1,128)S(1)}, u32[]{:S(2)}) copy-start(f32[1,1,256]{2,1,0:T(1,128)S(1)} %get-tuple-element.645) | copy-start | bytes 3076
  114.7 122.5 %copy-start.42 = (f32[1,1,256]{2,1,0:T(1,128)}, f32[1,1,256]{2,1,0:T(1,128)S(1)}, u32[]{:S(2)}) copy-start(f32[1,1,256]{2,1,0:T(1,128)S(1)} %get-tuple-element.646) | copy-start | bytes 3076
  114.7 122.5 %copy-start.44 = (f32[1,1,256]{2,1,0:T(1,128)}, f32[1,1,256]{2,1,0:T(1,128)S(1)}, u32[]{:S(2)}) copy-start(f32[1,1,256]{2,1,0:T(1,128)S(1)} %get-tuple-element.647) | copy-start | bytes 3076
  114.8 122.5 %copy-start.46 = (f32[1,1,256]{2,1,0:T(1,128)}, f32[1,1,256]{2,1,0:T(1,128)S(1)}, u32[]{:S(2)}) copy-start(f32[1,1,256]{2,1,0:T(1,128)S(1)} %get-tuple-element.648) | copy-start | bytes 3076
  264.1 24.0 %copy-start.7 = (f32[16,256]{1,0:T(8,128)S(1)}, f32[16,256]{1,0:T(8,128)}, u32[]{:S(2)}) copy-start(f32[16,256]{1,0:T(8,128)} %get-tuple-element.435) | copy-start | bytes 49156
  310.3 6.7 %copy-start.1 = (f32[256,128]{1,0:T(8,128)S(1)}, f32[256,128]{1,0:T(8,128)}, u32[]{:S(2)}) copy-start(f32[256,128]{1,0:T(8,128)} %reduce-scatter.2.cloned.1.call-done) | copy-start | bytes 393220
  310.3 15.6 %copy-start.35 = (f32[1,1,256]{2,1,0:T(1,128)S(1)}, f32[1,1,256]{2,1,0:T(1,128)}, u32[]{:S(2)}) copy-start(f32[1,1,256]{2,1,0:T(1,128)} %copy-done.34) | copy-start | bytes 3076
  310.3 15.6 %copy-start.37 = (f32[1,1,256]{2,1,0:T(1,128)S(1)}, f32[1,1,256]{2,1,0:T(1,128)}, u32[]{:S(2)}) copy-start(f32[1,1,256]{2,1,0:T(1,128)} %copy-done.36) | copy-start | bytes 3076
  310.3 15.6 %copy-start.39 = (f32[1,1,256]{2,1,0:T(1,128)S(1)}, f32[1,1,256]{2,1,0:T(1,128)}, u32[]{:S(2)}) copy-start(f32[1,1,256]{2,1,0:T(1,128)} %copy-done.38) | copy-start | bytes 3076
  310.3 15.6 %copy-start.41 = (f32[1,1,256]{2,1,0:T(1,128)S(1)}, f32[1,1,256]{2,1,0:T(1,128)}, u32[]{:S(2)}) copy-start(f32[1,1,256]{2,1,0:T(1,128)} %copy-done.40) | copy-start | bytes 3076
  310.3 15.6 %copy-start.43 = (f32[1,1,256]{2,1,0:T(1,128)S(1)}, f32[1,1,256]{2,1,0:T(1,128)}, u32[]{:S(2)}) copy-start(f32[1,1,256]{2,1,0:T(1,128)} %copy-done.42) | copy-start | bytes 3076
  310.4 15.6 %copy-start.45 = (f32[1,1,256]{2,1,0:T(1,128)S(1)}, f32[1,1,256]{2,1,0:T(1,128)}, u32[]{:S(2)}) copy-start(f32[1,1,256]{2,1,0:T(1,128)} %copy-done.44) | copy-start | bytes 3076
  310.4 15.6 %copy-start.47 = (f32[1,1,256]{2,1,0:T(1,128)S(1)}, f32[1,1,256]{2,1,0:T(1,128)}, u32[]{:S(2)}) copy-start(f32[1,1,256]{2,1,0:T(1,128)} %copy-done.46) | copy-start | bytes 3076
  317.1 8.7 %collective-permute-start.1 = (f32[3,6,256]{1,2,0:T(8,128)S(1)}, f32[3,6,256]{1,2,0:T(8,128)S(1)}, u32[]{:S(2)}, u32[]{:S(2)}) collective-permute-start(f32[3,6,256]{1,2,0:T(8,128)S(1)} %pad_maximum_fusion.1), channel_id=1, source_target_pairs={{32,0},{64,32},{96,64},{128,96},{160,128},{192,160},{224,192},{33,... | collective-permute-start | bytes 55304 | tf_op jit(solution)/shard_map/ppermute | solution.py:13
  325.8 28.7 %copy-start.20 = (f32[1,1,256]{2,1,0:T(1,128)S(1)}, f32[1,1,256]{2,1,0:T(1,128)}, u32[]{:S(2)}) copy-start(f32[1,1,256]{2,1,0:T(1,128)} %copy-done.19) | copy-start | bytes 3076
  325.8 28.7 %copy-start.22 = (f32[1,1,256]{2,1,0:T(1,128)S(1)}, f32[1,1,256]{2,1,0:T(1,128)}, u32[]{:S(2)}) copy-start(f32[1,1,256]{2,1,0:T(1,128)} %copy-done.21) | copy-start | bytes 3076
  325.8 28.6 %copy-start.24 = (f32[1,1,256]{2,1,0:T(1,128)S(1)}, f32[1,1,256]{2,1,0:T(1,128)}, u32[]{:S(2)}) copy-start(f32[1,1,256]{2,1,0:T(1,128)} %copy-done.23) | copy-start | bytes 3076
  325.8 28.6 %copy-start.26 = (f32[1,1,256]{2,1,0:T(1,128)S(1)}, f32[1,1,256]{2,1,0:T(1,128)}, u32[]{:S(2)}) copy-start(f32[1,1,256]{2,1,0:T(1,128)} %copy-done.25) | copy-start | bytes 3076
  326.4 30.0 %copy-start.10 = (f32[1,1,256]{2,1,0:T(1,128)S(1)}, f32[1,1,256]{2,1,0:T(1,128)}, u32[]{:S(2)}) copy-start(f32[1,1,256]{2,1,0:T(1,128)} %copy-done.9) | copy-start | bytes 3076
  326.4 30.0 %copy-start.12 = (f32[1,1,256]{2,1,0:T(1,128)S(1)}, f32[1,1,256]{2,1,0:T(1,128)}, u32[]{:S(2)}) copy-start(f32[1,1,256]{2,1,0:T(1,128)} %copy-done.11) | copy-start | bytes 3076
  326.5 29.9 %copy-start.14 = (f32[1,1,256]{2,1,0:T(1,128)S(1)}, f32[1,1,256]{2,1,0:T(1,128)}, u32[]{:S(2)}) copy-start(f32[1,1,256]{2,1,0:T(1,128)} %copy-done.13) | copy-start | bytes 3076
  326.5 29.9 %copy-start.16 = (f32[1,1,256]{2,1,0:T(1,128)S(1)}, f32[1,1,256]{2,1,0:T(1,128)}, u32[]{:S(2)}) copy-start(f32[1,1,256]{2,1,0:T(1,128)} %copy-done.15) | copy-start | bytes 3076
  326.5 29.9 %copy-start.18 = (f32[1,1,256]{2,1,0:T(1,128)S(1)}, f32[1,1,256]{2,1,0:T(1,128)}, u32[]{:S(2)}) copy-start(f32[1,1,256]{2,1,0:T(1,128)} %copy-done.17) | copy-start | bytes 3076
  326.5 29.9 %copy-start.31 = (f32[1,1,256]{2,1,0:T(1,128)S(1)}, f32[1,1,256]{2,1,0:T(1,128)}, u32[]{:S(2)}) copy-start(f32[1,1,256]{2,1,0:T(1,128)} %copy-done.30) | copy-start | bytes 3076
  326.5 29.9 %copy-start.33 = (f32[1,1,256]{2,1,0:T(1,128)S(1)}, f32[1,1,256]{2,1,0:T(1,128)}, u32[]{:S(2)}) copy-start(f32[1,1,256]{2,1,0:T(1,128)} %copy-done.32) | copy-start | bytes 3076
  328.3 75.4 %all-to-all-start = ((bf16[32,128,256]{1,2,0:T(8,128)(2,1)}), bf16[32,128,256]{1,2,0:T(8,128)(2,1)S(1)}, u32[]{:S(2)}, u32[]{:S(2)}) async-start(bf16[32,128,256]{1,2,0:T(8,128)(2,1)} %stack.22), calls=%async_computation.1 | async-start | bytes 4194304 | tf_op jit(solution)/shard_map/all_to_all | solution.py:160
Sparse Core Ops, SparseCore 0:
  9.8 95.8 all-gather.4
  111.3 124.2 reduce-scatter.1
